TPU v7x, 256 devices: a whole 4x4x8 slice. The times are simulated.
256 devices in a mesh: dp: 8 (over x, core), expert: 32 (over y, z).
Axes of the slice: x: 4, y: 4, z: 8, core: 2. Of those that a mesh axis runs over, the one named last changes fastest.
Arguments:
- tokens: bfloat16 [4096, 3584], P('expert'), may hold values from -6 to 6
- cotangent: bfloat16 [4096, 3584], P('expert'), may hold values from -0.59765625 to 0.59765625
- route_ids: int32 [4096, 8], P('expert'), may hold values from 0 to 31, all different within a row; in each aligned block of 128 rows (0 to 127, 128 to 255, ...) at most 40 rows name the same one
- route_gates: float32 [4096, 8], P('expert'), may hold values from 0.02 to 0.5
- w_gate: bfloat16 [32, 1792, 3584], P('expert', 'dp'), may hold values from -0.09375 to 0.09375
- w_up: bfloat16 [32, 1792, 3584], P('expert', 'dp'), may hold values from -0.09375 to 0.09375
- w_down: bfloat16 [32, 1792, 3584], P('expert', 'dp'), may hold values from -0.125 to 0.125
Outputs:
- layer_out: bfloat16 [4096, 3584], P(('expert', 'dp'))
- gate_grad: float32 [4096, 8], P(('expert', 'dp'))
- grad_w_gate: bfloat16 [32, 1792, 3584], P('expert', 'dp')
- grad_w_up: bfloat16 [32, 1792, 3584], P('expert', 'dp')
- grad_w_down: bfloat16 [32, 1792, 3584], P('expert', 'dp')
Inputs may be any that keep to these rules, and one draw needn't show every extreme that they name: `route_ids`: each row names 8 different experts. Within each aligned block of 128 rows (the tokens of one index of expert) no expert is named more than 40 times, a bound that some block reaches.
All inputs are finite; a program needn't handle non-finite values.
Results may differ from a plain program's by a relative error of at most 0.02.
Values may be sent and summed in bfloat16 or wider, within the bound.
No kernel may reach another device: no remote copies, remote signals or barrier semaphores. Data moves between devices by JAX's collectives and lax.ppermute only.
A program may use at most 128 MiB of HBM per device.

v0:
```python
import jax
import jax.numpy as jnp
from jax import lax
from jax.sharding import PartitionSpec as P


def body(tokens, cotangent, route_ids, route_gates, w_gate, w_up, w_down):
    groups = lax.axis_size("expert")
    dp_count = lax.axis_size("dp")
    dp_idx = lax.axis_index("dp")
    tok_rows, width = tokens.shape
    top_slots = route_ids.shape[1]
    cap_rows = min(tok_rows, dp_count * max(1, tok_rows * top_slots * 5 // (4 * groups * dp_count)))
    share = cap_rows // dp_count
    n_dest = groups * share
    flat_ids = route_ids.reshape(-1)
    onehot = (flat_ids[:, None] == jnp.arange(groups, dtype=jnp.int32)[None, :]).astype(jnp.int32)
    n_slots = flat_ids.shape[0]
    lower = (
        jnp.arange(n_slots, dtype=jnp.int32)[:, None]
        >= jnp.arange(n_slots, dtype=jnp.int32)[None, :]
    ).astype(jnp.bfloat16)
    running = jnp.dot(lower, onehot.astype(jnp.bfloat16), preferred_element_type=jnp.float32)
    slot_rank = jnp.sum(running.astype(jnp.int32) * onehot, axis=1) - 1
    local_rank = slot_rank - dp_idx * share
    mine = (local_rank >= 0) & (local_rank < share)
    dest = jnp.where(mine, local_rank * groups + flat_ids, n_dest)
    dest_hot = (dest[:, None] == jnp.arange(n_dest, dtype=jnp.int32)[None, :]).astype(jnp.float32)
    pick = jnp.sum(dest_hot.reshape(tok_rows, top_slots, n_dest), axis=1).T
    pick_bf = pick.astype(jnp.bfloat16)
    gate_sel = jnp.sum(dest_hot * route_gates.reshape(-1)[:, None], axis=0)
    send_x = jnp.dot(pick_bf, tokens, preferred_element_type=jnp.float32).astype(jnp.bfloat16)
    cot_sel = jnp.dot(pick_bf, cotangent, preferred_element_type=jnp.float32)
    send_dy = (gate_sel[:, None] * cot_sel).astype(jnp.bfloat16)

    def to_lanes(rows):
        return jnp.concatenate([rows[r * groups : (r + 1) * groups] for r in range(share)], axis=1)

    def lanes_to_rows(packed):
        return jnp.concatenate(
            [packed[:, r * width : (r + 1) * width] for r in range(share)], axis=0
        )

    recv_x = lax.all_to_all(to_lanes(send_x), "expert", split_axis=0, concat_axis=0, tiled=True)
    recv_x, lanes_dy = lax.optimization_barrier((recv_x, to_lanes(send_dy)))
    recv_dy = lax.all_to_all(lanes_dy, "expert", split_axis=0, concat_axis=0, tiled=True)
    gathered_x = lax.all_gather(recv_x, "dp", axis=0, tiled=True)
    x_chunks = [gathered_x[:, r * width : (r + 1) * width] for r in range(share)]
    gate_local = w_gate[0]
    up_local = w_up[0]
    down_local = w_down[0]
    by_feature = (((1,), (1,)), ((), ()))
    by_row = (((0,), (0,)), ((), ()))
    gate_pre = jnp.concatenate(
        [
            lax.dot_general(xc, gate_local, by_feature, preferred_element_type=jnp.float32)
            for xc in x_chunks
        ],
        axis=0,
    )
    up_pre = jnp.concatenate(
        [
            lax.dot_general(xc, up_local, by_feature, preferred_element_type=jnp.float32)
            for xc in x_chunks
        ],
        axis=0,
    )
    sigma_gate = jax.nn.sigmoid(gate_pre)
    hidden = (gate_pre * sigma_gate * up_pre).astype(jnp.bfloat16)
    stack_rows = dp_count * groups
    y_lanes = jnp.concatenate(
        [
            jnp.dot(
                hidden[r * stack_rows : (r + 1) * stack_rows],
                down_local,
                preferred_element_type=jnp.float32,
            ).astype(jnp.bfloat16)
            for r in range(share)
        ],
        axis=1,
    )
    flat_x = jnp.concatenate(x_chunks, axis=0)
    y_sum = lax.psum_scatter(y_lanes, "dp", scatter_dimension=0, tiled=True)
    y_sum, recv_dy = lax.optimization_barrier((y_sum, recv_dy))
    flat_dy = lanes_to_rows(lax.all_gather(recv_dy, "dp", axis=0, tiled=True))
    y_back = lax.all_to_all(y_sum, "expert", split_axis=0, concat_axis=0, tiled=True)
    y_back, flat_dy = lax.optimization_barrier((y_back, flat_dy))
    y_home = lanes_to_rows(y_back).astype(jnp.float32)
    hidden_grad = lax.dot_general(
        flat_dy, down_local, by_feature, preferred_element_type=jnp.float32
    )
    grad_gate_pre = (
        hidden_grad * up_pre * sigma_gate * (1.0 + gate_pre * (1.0 - sigma_gate))
    ).astype(jnp.bfloat16)
    grad_up_pre = (hidden_grad * gate_pre * sigma_gate).astype(jnp.bfloat16)
    grad_down = lax.dot_general(hidden, flat_dy, by_row, preferred_element_type=jnp.float32)
    grad_gate = lax.dot_general(grad_gate_pre, flat_x, by_row, preferred_element_type=jnp.float32)
    grad_up = lax.dot_general(grad_up_pre, flat_x, by_row, preferred_element_type=jnp.float32)
    out_part = lax.dot_general(
        pick,
        gate_sel[:, None] * y_home,
        by_row,
        precision=lax.Precision.HIGHEST,
        preferred_element_type=jnp.float32,
    )
    dot_dest = jnp.sum(cot_sel * y_home, axis=1)
    grad_part = jnp.sum(dest_hot * dot_dest[None, :], axis=1).reshape(tok_rows, top_slots)
    both_sum = lax.psum_scatter(
        jnp.concatenate([out_part, grad_part], axis=1).astype(jnp.bfloat16),
        "dp",
        scatter_dimension=0,
        tiled=True,
    )
    layer_sum = both_sum[:, :width]
    gate_sum = both_sum[:, width:].astype(jnp.float32)
    return (
        layer_sum.astype(jnp.bfloat16),
        gate_sum,
        grad_gate.astype(jnp.bfloat16)[None],
        grad_up.astype(jnp.bfloat16)[None],
        grad_down.astype(jnp.bfloat16)[None],
    )


def solution(mesh):
    return jax.shard_map(
        body,
        mesh=mesh,
        in_specs=(
            P("expert", None),
            P("expert", None),
            P("expert", None),
            P("expert", None),
            P("expert", "dp", None),
            P("expert", "dp", None),
            P("expert", "dp", None),
        ),
        out_specs=(
            P(("expert", "dp"), None),
            P(("expert", "dp"), None),
            P("expert", "dp", None),
            P("expert", "dp", None),
            P("expert", "dp", None),
        ),
        check_vma=False,
    )
```

profile of v0, /device:TPU:8, one launch (start us, length us, event | category | flops | bytes accessed | tf_op | source)
XLA Modules:
  0.0 315.9 jit_solution(5336384310232286521)
XLA Ops:
  7.2 0.9 copy.32
  9.8 1.0 copy-done.3
  11.3 2.8 reduce
  14.0 1.2 reshape.61
  15.2 11.8 %all-to-all-start = ((bf16[32,2,8960]{2,1,0:T(2,128)(2,1)}), bf16[32,2,8960]{2,1,0:T(2,128)(2,1)S(1)}, u32[]{:S(2)}, u32[]{:S(2)}) async-start(bf16[32,2,8960]{2,1,0:T(2,128)(2,1)} %reshape.61), calls=%async_computation | async-start | bytes 2293760 | tf_op jit(solution)/shard_map/all_to_all | solution.py:44
  27.4 3.0 multiply_convert_fusion
  30.5 0.7 slice_dynamic-update-slice_fusion.14
  31.2 0.7 slice_dynamic-update-slice_fusion.13
  31.9 0.7 slice_dynamic-update-slice_fusion.12
  32.6 0.7 slice_dynamic-update-slice_fusion.11
  33.3 0.7 slice_dynamic-update-slice_fusion.10
  34.0 21.2 %all-to-all-done = bf16[32,2,8960]{2,1,0:T(2,128)(2,1)S(1)} async-done(((bf16[32,2,8960]{2,1,0:T(2,128)(2,1)}), bf16[32,2,8960]{2,1,0:T(2,128)(2,1)S(1)}, u32[]{:S(2)}, u32[]{:S(2)}) %all-to-all-start) | async-done | bytes 1146912 | tf_op jit(solution)/shard_map/all_to_all | solution.py:44
  55.1 3.4 %reshape.62 = bf16[32,1,17920]{2,1,0:T(2,128)(2,1)} reshape(bf16[32,2,8960]{2,1,0:T(2,128)(2,1)S(1)} %all-to-all-done) | data formatting | bytes 2293760
  58.6 2.9 copy.48
  61.5 54.5 %all-gather.3.cloned.1.call-done = bf16[256,17920]{1,0:T(8,128)(2,1)} async-done(((bf16[32,17920]{1,0:T(8,128)(2,1)}), bf16[256,17920]{1,0:T(8,128)(2,1)}) %all-gather.3.cloned.1.call-update) | async-done | bytes 9175056 | tf_op jit(solution)/shard_map/all_gather | solution.py:47
  116.0 2.4 fusion.72
  118.4 2.7 fusion.77
  121.1 2.2 fusion.82
  123.3 0.7 fusion.87
  124.0 0.7 fusion.92
  124.8 0.7 copy-done.13
  125.5 0.7 fusion.47
  126.2 0.7 fusion.52
  126.9 0.7 fusion.57
  127.6 0.7 fusion.62
  128.3 0.7 fusion.67
  129.4 1.9 fusion.4
  131.3 1.9 fusion.3
  133.2 1.9 fusion.2
  135.1 1.9 fusion.1
  137.1 2.0 fusion
  139.1 2.8 reduce.1
  141.9 1.2 reshape.63
  143.0 41.6 %all_to_all.36 = bf16[32,2,8960]{2,1,0:T(2,128)(2,1)S(1)} all-to-all(bf16[32,2,8960]{2,1,0:T(2,128)(2,1)} %reshape.63), channel_id=1, replica_groups=mesh['dp'=8,'expert'=32] {'expert'}, dimensions={0} | all-to-all | bytes 2293760 | tf_op jit(solution)/shard_map/all_to_all | solution.py:46
  184.6 3.4 %reshape.64 = bf16[32,1,17920]{2,1,0:T(2,128)(2,1)} reshape(bf16[32,2,8960]{2,1,0:T(2,128)(2,1)S(1)} %all_to_all.36) | data formatting | bytes 2293760
  188.0 2.9 copy.47
  190.9 7.3 %reduce-scatter.3.cloned.1.call-done = bf16[32,17920]{1,0:T(8,128)(2,1)} async-done(((bf16[256,17920]{1,0:T(8,128)(2,1)}), bf16[32,17920]{1,0:T(8,128)(2,1)}) %reduce-scatter.3.cloned.1.call-update) | async-done | bytes 1146896 | tf_op jit(solution)/shard_map/reduce_scatter | solution.py:83
  198.2 1.6 slice_dynamic-update-slice_fusion.9
  199.8 1.6 slice_dynamic-update-slice_fusion.8
  201.5 3.6 %copy-done.9 = bf16[1280,3584]{1,0:T(8,128)(2,1)} copy-done((bf16[1280,3584]{1,0:T(8,128)(2,1)}, bf16[1280,3584]{1,0:T(8,128)(2,1)S(1)}, u32[]{:S(2)}) %copy-start.9) | copy-done | bytes 9175064
  205.1 2.8 reduce.2
  207.9 1.2 reshape.65
  209.0 10.1 %all-to-all-start.2 = ((bf16[32,2,8960]{2,1,0:T(2,128)(2,1)}), bf16[32,2,8960]{2,1,0:T(2,128)(2,1)S(1)}, u32[]{:S(2)}, u32[]{:S(2)}) async-start(bf16[32,2,8960]{2,1,0:T(2,128)(2,1)} %reshape.65), calls=%async_computation.3 | async-start | bytes 2293760 | tf_op jit(solution)/shard_map/all_to_all | solution.py:86
  219.2 2.9 slice_dynamic-update-slice_fusion.7
  222.1 3.0 slice_dynamic-update-slice_fusion.6
  225.1 2.9 slice_dynamic-update-slice_fusion.5
  228.0 18.9 %all-to-all-done.2 = bf16[32,2,8960]{2,1,0:T(2,128)(2,1)S(1)} async-done(((bf16[32,2,8960]{2,1,0:T(2,128)(2,1)}), bf16[32,2,8960]{2,1,0:T(2,128)(2,1)S(1)}, u32[]{:S(2)}, u32[]{:S(2)}) %all-to-all-start.2) | async-done | bytes 1146912 | tf_op jit(solution)/shard_map/all_to_all | solution.py:86
  247.0 3.4 %reshape.66 = bf16[32,1,17920]{2,1,0:T(2,128)(2,1)} reshape(bf16[32,2,8960]{2,1,0:T(2,128)(2,1)S(1)} %all-to-all-done.2) | data formatting | bytes 2293760
  250.4 1.8 copy.46
  252.1 3.6 %all-gather.5.cloned.1.call-done = bf16[256,17920]{1,0:T(8,128)(2,1)} async-done(((bf16[32,17920]{1,0:T(8,128)(2,1)}), bf16[256,17920]{1,0:T(8,128)(2,1)}) %all-gather.5.cloned.1.call-update) | async-done | bytes 9175056 | tf_op jit(solution)/shard_map/all_gather | solution.py:85
  255.8 1.6 slice_dynamic-update-slice_fusion.4
  257.4 1.6 slice_dynamic-update-slice_fusion.3
  259.0 1.6 slice_dynamic-update-slice_fusion.2
  260.6 1.6 slice_dynamic-update-slice_fusion.1
  262.3 1.6 slice_dynamic-update-slice_fusion
  263.9 4.0 %fusion.10 = f32[1280,224]{0,1:T(8,128)} fusion(bf16[1280,3584]{1,0:T(8,128)(2,1)S(1)} %slice_dynamic-update-slice_fusion, bf16[1,224,3584]{2,1,0:T(8,128)(2,1)S(1)} %copy-done), kind=kOutput, calls=%fused_computation.29 | convolution fusion | flops 2055208960 | bytes 11927552 | tf_op jit(solution)/shard_map/dot_general | solution.py:89
  268.0 1.9 convolution_convert_fusion.9
  270.5 1.0 pad_maximum_fusion
  271.6 7.2 %fusion.7 = bf16[1,224,3584]{2,1,0:T(8,128)(2,1)} fusion(bf16[1280,224]{0,1:T(8,128)(2,1)S(1)} %multiply_convert_fusion.3, bf16[1280,3584]{1,0:T(8,128)(2,1)} %copy-done.10), kind=kOutput, calls=%fused_computation.16 | convolution fusion | flops 2056011776 | bytes 11354112 | tf_op jit(solution)/shard_map/dot_general | solution.py:96
  278.8 3.5 %fusion.6 = bf16[1,224,3584]{2,1,0:T(8,128)(2,1)} fusion(bf16[1280,3584]{1,0:T(8,128)(2,1)S(1)} %bitcast.91, f32[1280,224]{0,1:T(8,128)S(1)} %copy-done.14, f32[1280,224]{0,1:T(8,128)S(1)} %copy-done.7), kind=kOutput, calls=%fused_computation.15 | convolution fusion | flops 2057732096 | bytes 13074432 | tf_op jit(solution)/shard_map/dot_general | solution.py:98
  282.3 3.7 %fusion.5 = bf16[1,224,3584]{2,1,0:T(8,128)(2,1)} fusion(bf16[1280,3584]{1,0:T(8,128)(2,1)S(1)} %bitcast.91, f32[1280,224]{0,1:T(8,128)S(1)} %copy-done.7, f32[1280,224]{0,1:T(8,128)S(1)} %copy-done.14, f32[1280,224]{0,1:T(8,128)S(1)} %copy-done.5), kind=kOutput, calls=%fused_computation.14 | convolution fusion | flops 2058878976 | bytes 14221312 | tf_op jit(solution)/shard_map/dot_general | solution.py:97
  286.0 20.5 %reduce-scatter.5.cloned.1.call-done = bf16[16,3592]{1,0:T(8,128)(2,1)} async-done(((bf16[128,3592]{1,0:T(8,128)(2,1)}), bf16[16,3592]{1,0:T(8,128)(2,1)}) %reduce-scatter.5.cloned.1.call-update) | async-done | bytes 114960 | tf_op jit(solution)/shard_map/reduce_scatter | solution.py:108
  306.5 0.7 slice_convert_fusion
  307.8 1.6 slice.153
  (70 shorter events, 4.3 us)
Async XLA Ops:
  7.2 122.2 %copy-start = (bf16[1,224,3584]{2,1,0:T(8,128)(2,1)S(1)}, bf16[1,224,3584]{2,1,0:T(8,128)(2,1)}, u32[]{:S(2)}) copy-start(bf16[1,224,3584]{2,1,0:T(8,128)(2,1)} %param.13) | copy-start | bytes 4816900
  7.2 2.0 copy-start.8
  9.7 1.0 copy-start.3
  15.2 11.9 %copy-start.11 = (f32[128,8]{0,1:T(8,128)S(1)}, f32[128,8]{0,1:T(8,128)}, u32[]{:S(2)}) copy-start(f32[128,8]{0,1:T(8,128)} %param.10) | copy-start | bytes 12292
  15.2 40.0 %all-to-all-start = ((bf16[32,2,8960]{2,1,0:T(2,128)(2,1)}), bf16[32,2,8960]{2,1,0:T(2,128)(2,1)S(1)}, u32[]{:S(2)}, u32[]{:S(2)}) async-start(bf16[32,2,8960]{2,1,0:T(2,128)(2,1)} %reshape.61), calls=%async_computation | async-start | bytes 2293760 | tf_op jit(solution)/shard_map/all_to_all | solution.py:44
  27.0 89.0 %all-gather.3.cloned.1.call-start = ((), (), s32[]{:S(2)}) async-start(), calls=%async_computation.5 | async-start | bytes 10321920 | tf_op jit(solution)/shard_map/all_gather | solution.py:47
  58.6 57.4 %copy-start.12 = (bf16[1,224,3584]{2,1,0:T(8,128)(2,1)S(1)}, bf16[1,224,3584]{2,1,0:T(8,128)(2,1)}, u32[]{:S(2)}) copy-start(bf16[1,224,3584]{2,1,0:T(8,128)(2,1)} %param.12) | copy-start | bytes 4816900
  61.5 136.7 %reduce-scatter.3.cloned.1.call-start = ((), (), s32[]{:S(2)}) async-start(), calls=%async_computation.6 | async-start | bytes 10321920 | tf_op jit(solution)/shard_map/reduce_scatter | solution.py:83
  116.0 7.3 %copy-start.1 = (bf16[256,17920]{1,0:T(8,128)(2,1)S(1)}, bf16[256,17920]{1,0:T(8,128)(2,1)}, u32[]{:S(2)}) copy-start(bf16[256,17920]{1,0:T(8,128)(2,1)} %all-gather.3.cloned.1.call-done) | copy-start | bytes 27525124
  124.0 1.4 copy-start.13
  125.5 3.6 %copy-start.4 = (f32[1280,224]{0,1:T(8,128)}, f32[1280,224]{0,1:T(8,128)S(1)}, u32[]{:S(2)}) copy-start(f32[1280,224]{0,1:T(8,128)S(1)} %fusion.92) | copy-start | bytes 3440644
  129.0 2.3 copy-start.6
  139.0 116.7 %all-gather.5.cloned.1.call-start = ((), (), s32[]{:S(2)}) async-start(), calls=%async_computation.7 | async-start | bytes 10321920 | tf_op jit(solution)/shard_map/all_gather | solution.py:85
  201.5 3.6 %copy-start.9 = (bf16[1280,3584]{1,0:T(8,128)(2,1)}, bf16[1280,3584]{1,0:T(8,128)(2,1)S(1)}, u32[]{:S(2)}) copy-start(bf16[1280,3584]{1,0:T(8,128)(2,1)S(1)} %slice_dynamic-update-slice_fusion.8) | copy-start | bytes 27525124
  209.0 37.9 %all-to-all-start.2 = ((bf16[32,2,8960]{2,1,0:T(2,128)(2,1)}), bf16[32,2,8960]{2,1,0:T(2,128)(2,1)S(1)}, u32[]{:S(2)}, u32[]{:S(2)}) async-start(bf16[32,2,8960]{2,1,0:T(2,128)(2,1)} %reshape.65), calls=%async_computation.3 | async-start | bytes 2293760 | tf_op jit(solution)/shard_map/all_to_all | solution.py:86
  219.2 87.3 %reduce-scatter.5.cloned.1.call-start = ((), (), s32[]{:S(2)}) async-start(), calls=%async_computation.8 | async-start | bytes 1069056 | tf_op jit(solution)/shard_map/reduce_scatter | solution.py:108
  263.9 4.0 %copy-start.10 = (bf16[1280,3584]{1,0:T(8,128)(2,1)}, bf16[1280,3584]{1,0:T(8,128)(2,1)S(1)}, u32[]{:S(2)}) copy-start(bf16[1280,3584]{1,0:T(8,128)(2,1)S(1)} %slice_dynamic-update-slice_fusion) | copy-start | bytes 27525124
  268.0 1.9 copy-start.2
  271.5 7.2 %slice-start = ((s8[9175040]{0:T(1024)(128)(4,1)}), s8[786432]{0:T(1024)(128)(4,1)S(1)}, s32[]{:S(2)}) async-start(s8[9175040]{0:T(1024)(128)(4,1)} %bitcast.90), calls=%async_computation.9 | async-start | bytes 1572864
  271.5 7.2 %copy-start.7 = (f32[1280,224]{0,1:T(8,128)S(1)}, f32[1280,224]{0,1:T(8,128)}, u32[]{:S(2)}) copy-start(f32[1280,224]{0,1:T(8,128)} %copy-done.6) | copy-start | bytes 3440644
  271.6 7.2 %slice-start.1 = ((s8[9175040]{0:T(1024)(128)(4,1)}), s8[4194304]{0:T(1024)(128)(4,1)S(1)}, s32[]{:S(2)}) async-start(s8[9175040]{0:T(1024)(128)(4,1)} %bitcast.90), calls=%async_computation.10 | async-start | bytes 8388608
  271.6 7.2 %slice-start.2 = ((s8[9175040]{0:T(1024)(128)(4,1)}), s8[4194304]{0:T(1024)(128)(4,1)S(1)}, s32[]{:S(2)}) async-start(s8[9175040]{0:T(1024)(128)(4,1)} %bitcast.90), calls=%async_computation.11 | async-start | bytes 8388608
  271.6 7.2 %copy-start.14 = (f32[1280,224]{0,1:T(8,128)S(1)}, f32[1280,224]{0,1:T(8,128)}, u32[]{:S(2)}) copy-start(f32[1280,224]{0,1:T(8,128)} %fusion.10) | copy-start | bytes 3440644
  278.8 3.5 %copy-start.5 = (f32[1280,224]{0,1:T(8,128)S(1)}, f32[1280,224]{0,1:T(8,128)}, u32[]{:S(2)}) copy-start(f32[1280,224]{0,1:T(8,128)} %copy-done.4) | copy-start | bytes 3440644
Sparse Core Ops, SparseCore 0:
  61.6 54.3 all-gather.2
  139.2 58.9 reduce-scatter.2
  200.6 55.1 all-gather.4
  271.7 34.7 reduce-scatter.4
where the time goes:
time: 317 us; the launch traced here: 316 us
  waiting for transfers between devices  126 us (40%)
  local copies, waits for them, and re-layouts  54.7 us (17%)
  matrix products  46.1 us (15%)
  blocking collectives  41.6 us (13%)
  starting transfers between devices  22.1 us (7%)
  between operations  14.3 us (5%)
  other arithmetic  11.1 us (4%)
    all_gather x1, waiting for transfers between devices, body(): gathered_x = lax.all_gather(recv_x, 'dp', axis=0, tiled=True)  54.5 us
    unnamed x68, local copies, waits for them, and re-layouts  46.8 us
    all_to_all x1, blocking collectives, body(): lax.all_to_all(lanes_dy, 'expert', split_axis=0, concat_axis=0, tiled=True)  41.6 us
    all_to_all x1, waiting for transfers between devices, body(): lax.all_to_all(to_lanes(send_x), 'expert', split_axis=0, concat_axis=0, t...  21.2 us
    reduce_scatter x1, waiting for transfers between devices, body(): lax.psum_scatter(jnp.concatenate([out_part, grad_part], axis=1).astype(jn...  20.5 us
    all_to_all x1, waiting for transfers between devices, body(): lax.all_to_all(y_sum, 'expert', split_axis=0, concat_axis=0, tiled=True)  18.9 us
    all_to_all x1, starting transfers between devices, body(): lax.all_to_all(to_lanes(send_x), 'expert', split_axis=0, concat_axis=0, t...  11.8 us
    all_to_all x1, starting transfers between devices, body(): lax.all_to_all(y_sum, 'expert', split_axis=0, concat_axis=0, tiled=True)  10.1 us
  transfers between devices with their start and end apart: 6, of which 6 were waited for; matrix products, arithmetic and copies ran while one was open for 17% of the time, Pallas kernels for 0%

commit v1 on v0

--- a/solution.py
+++ b/solution.py
@@ -2,6 +2,12 @@
 import jax.numpy as jnp
 from jax import lax
 from jax.sharding import PartitionSpec as P
+
+
+def in_order(blocks, dim):
+    shape = list(blocks.shape[1:])
+    shape[dim] *= blocks.shape[0]
+    return jnp.moveaxis(blocks, 0, dim).reshape(shape)
 
 
 def body(tokens, cotangent, route_ids, route_gates, w_gate, w_up, w_down):
@@ -44,7 +50,19 @@
     recv_x = lax.all_to_all(to_lanes(send_x), "expert", split_axis=0, concat_axis=0, tiled=True)
     recv_x, lanes_dy = lax.optimization_barrier((recv_x, to_lanes(send_dy)))
     recv_dy = lax.all_to_all(lanes_dy, "expert", split_axis=0, concat_axis=0, tiled=True)
-    gathered_x = lax.all_gather(recv_x, "dp", axis=0, tiled=True)
+    size = lax.axis_size("dp")
+    pairs = [(i, (i + 1) % size) for i in range(size)]
+    back = [(b, a) for a, b in pairs]
+    lower_2, upper = ([], [])
+    for step in range(size - 1):
+        if step % 2 == 0:
+            lower_2.append(lax.ppermute(lower_2[-1] if lower_2 else recv_x, "dp", pairs))
+        else:
+            upper.append(lax.ppermute(upper[-1] if upper else recv_x, "dp", back))
+    blocks = jnp.stack([*lower_2[::-1], recv_x, *upper])
+    shift = lax.axis_index("dp") - len(lower_2)
+    blocks = blocks[(jnp.arange(size) - shift) % size]
+    gathered_x = in_order(blocks, 0)
     x_chunks = [gathered_x[:, r * width : (r + 1) * width] for r in range(share)]
     gate_local = w_gate[0]
     up_local = w_up[0]

time: 317 us -> 349 us (1.10)
  local copies, waits for them, and re-layouts: 54.7 us -> 76.6 us
  starting transfers between devices: 22.1 us -> 31.4 us
  blocking collectives: 41.6 us -> 33.3 us
  waiting for transfers between devices: 126 us -> 133 us
    ppermute x0 -> x7, waiting for transfers between devices: none -> 57.2 us  [the longest x4 57.1 us: body(): lax.ppermute(lower_2[-1] if lower_2 else recv_x, 'dp', pairs)]
    all_gather x1 -> x0, waiting for transfers between devices: 54.5 us -> none  [body(): gathered_x = lax.all_gather(recv_x, 'dp', axis=0, tiled=True)]
    unnamed x68 -> x83, local copies, waits for them, and re-layouts: 46.8 us -> 59 us
    ppermute x0 -> x7, starting transfers between devices: none -> 9.14 us  [the longest x3 9.11 us: body(): upper.append(lax.ppermute(upper[-1] if upper else recv_x, 'dp', back))]
    gather x0 -> x1, local copies, waits for them, and re-layouts: none -> 8.68 us  [body(): blocks = blocks[(jnp.arange(size) - shift) % size]]
    all_to_all x1, blocking collectives: 41.6 us -> 33.3 us  [body(): lax.all_to_all(lanes_dy, 'expert', split_axis=0, concat_axis=0, tiled=True)]
    reduce_scatter x1, waiting for transfers between devices: 7.35 us -> 11.6 us  [body(): y_sum = lax.psum_scatter(y_lanes, 'dp', scatter_dimension=0, tiled=True)]
  transfers between devices with their start and end apart: 6 -> 12, of which waited for: 6 -> 10; matrix products, arithmetic and copies ran while one was open for 17% -> 19% of each run, Pallas kernels for 0% -> 0%
where the time goes in v1:
time: 349 us; the launch traced here: 348 us
  waiting for transfers between devices  133 us (38%)
  local copies, waits for them, and re-layouts  76.6 us (22%)
  matrix products  47.7 us (14%)
  blocking collectives  33.3 us (10%)
  starting transfers between devices  31.4 us (9%)
  between operations  14.3 us (4%)
  other arithmetic  11.1 us (3%)
    unnamed x83, local copies, waits for them, and re-layouts  59 us
    ppermute x4, waiting for transfers between devices, body(): lax.ppermute(lower_2[-1] if lower_2 else recv_x, 'dp', pairs)  57.1 us
    all_to_all x1, blocking collectives, body(): lax.all_to_all(lanes_dy, 'expert', split_axis=0, concat_axis=0, tiled=True)  33.3 us
    all_to_all x1, waiting for transfers between devices, body(): lax.all_to_all(to_lanes(send_x), 'expert', split_axis=0, concat_axis=0, t...  21.1 us
    reduce_scatter x1, waiting for transfers between devices, body(): lax.psum_scatter(jnp.concatenate([out_part, grad_part], axis=1).astype(jn...  20.5 us
    all_to_all x1, waiting for transfers between devices, body(): lax.all_to_all(y_sum, 'expert', split_axis=0, concat_axis=0, tiled=True)  18.9 us
    all_to_all x1, starting transfers between devices, body(): lax.all_to_all(to_lanes(send_x), 'expert', split_axis=0, concat_axis=0, t...  11.8 us
    reduce_scatter x1, waiting for transfers between devices, body(): y_sum = lax.psum_scatter(y_lanes, 'dp', scatter_dimension=0, tiled=True)  11.6 us
  transfers between devices with their start and end apart: 12, of which 10 were waited for; matrix products, arithmetic and copies ran while one was open for 19% of the time, Pallas kernels for 0%

profile of v1, /device:TPU:8, one launch (start us, length us, event | category | flops | bytes accessed | tf_op | source)
XLA Modules:
  0.0 347.5 jit_solution(1816224620301165280)
XLA Ops:
  9.8 1.0 copy-done.3
  11.3 2.8 reduce
  14.0 1.2 reshape.122
  15.2 11.8 %all-to-all-start = ((bf16[32,2,8960]{2,1,0:T(2,128)(2,1)}), bf16[32,2,8960]{2,1,0:T(2,128)(2,1)S(1)}, u32[]{:S(2)}, u32[]{:S(2)}) async-start(bf16[32,2,8960]{2,1,0:T(2,128)(2,1)} %reshape.122), calls=%async_computation | async-start | bytes 2293760 | tf_op jit(solution)/shard_map/all_to_all | solution.py:50
  27.4 3.1 multiply_convert_fusion
  34.0 21.1 %all-to-all-done = bf16[32,2,8960]{2,1,0:T(2,128)(2,1)S(1)} async-done(((bf16[32,2,8960]{2,1,0:T(2,128)(2,1)}), bf16[32,2,8960]{2,1,0:T(2,128)(2,1)S(1)}, u32[]{:S(2)}, u32[]{:S(2)}) %all-to-all-start) | async-done | bytes 1146912 | tf_op jit(solution)/shard_map/all_to_all | solution.py:50
  55.1 3.4 reshape.123
  58.5 1.8 copy.48
  60.3 16.5 %collective-permute-done = bf16[32,17920]{1,0:T(8,128)(2,1)S(1)} collective-permute-done((bf16[32,17920]{1,0:T(8,128)(2,1)S(1)}, bf16[32,17920]{1,0:T(8,128)(2,1)S(1)}, u32[]{:S(2)}, u32[]{:S(2)}) %collective-permute-start) | collective-permute-done | bytes 1146912 | tf_op jit(solution)/shard_map/ppermute | solution.py:59
  76.8 3.0 collective-permute-start.4
  79.8 13.5 %collective-permute-done.1 = bf16[32,17920]{1,0:T(8,128)(2,1)S(1)} collective-permute-done((bf16[32,17920]{1,0:T(8,128)(2,1)S(1)}, bf16[32,17920]{1,0:T(8,128)(2,1)S(1)}, u32[]{:S(2)}, u32[]{:S(2)}) %collective-permute-start.1) | collective-permute-done | bytes 1146912 | tf_op jit(solution)/shard_map/ppermute | solution.py:59
  93.3 3.0 collective-permute-start.5
  96.4 13.5 %collective-permute-done.2 = bf16[32,17920]{1,0:T(8,128)(2,1)} collective-permute-done((bf16[32,17920]{1,0:T(8,128)(2,1)S(1)}, bf16[32,17920]{1,0:T(8,128)(2,1)}, u32[]{:S(2)}, u32[]{:S(2)}) %collective-permute-start.2) | collective-permute-done | bytes 1146912 | tf_op jit(solution)/shard_map/ppermute | solution.py:59
  110.0 3.1 collective-permute-start.6
  113.2 13.5 %collective-permute-done.3 = bf16[32,17920]{1,0:T(8,128)(2,1)} collective-permute-done((bf16[32,17920]{1,0:T(8,128)(2,1)}, bf16[32,17920]{1,0:T(8,128)(2,1)}, u32[]{:S(2)}, u32[]{:S(2)}) %collective-permute-start.3) | collective-permute-done | bytes 1146912 | tf_op jit(solution)/shard_map/ppermute | solution.py:59
  126.7 2.3 bitcast_dynamic-update-slice_fusion.7
  129.0 2.4 bitcast_dynamic-update-slice_fusion.6
  131.5 1.1 bitcast_dynamic-update-slice_fusion.5
  133.1 1.2 bitcast_dynamic-update-slice_fusion.4
  134.3 1.1 bitcast_dynamic-update-slice_fusion.3
  135.4 2.4 bitcast_dynamic-update-slice_fusion.2
  137.7 2.3 bitcast_dynamic-update-slice_fusion.1
  140.1 1.1 bitcast_dynamic-update-slice_fusion
  141.2 8.7 %gather_fusion = bf16[8,32,17920]{2,1,0:T(8,128)(2,1)} fusion(bf16[8,32,17920]{2,1,0:T(8,128)(2,1)} %bitcast_dynamic-update-slice_fusion, s32[1024]{0:T(1024)S(1)} %pad_clamp_fusion), kind=kCustom, calls=%fused_computation | custom fusion | bytes 18350112 | tf_op jit(solution)/shard_map/gather | solution.py:64
  149.9 2.8 fusion.72
  152.7 3.2 fusion.77
  155.9 2.8 fusion.82
  164.8 2.0 fusion.4
  166.8 1.9 fusion.3
  168.7 1.9 fusion.2
  170.6 1.9 fusion.1
  172.6 1.9 fusion
  174.7 2.8 reduce.1
  177.5 1.2 reshape.124
  178.7 33.3 %all_to_all.36 = bf16[32,2,8960]{2,1,0:T(2,128)(2,1)S(1)} all-to-all(bf16[32,2,8960]{2,1,0:T(2,128)(2,1)} %reshape.124), channel_id=1, replica_groups=mesh['dp'=8,'expert'=32] {'expert'}, dimensions={0} | all-to-all | bytes 2293760 | tf_op jit(solution)/shard_map/all_to_all | solution.py:52
  212.0 3.4 reshape.125
  215.4 2.9 copy.47
  218.3 11.6 %reduce-scatter.3.cloned.1.call-done = bf16[32,17920]{1,0:T(8,128)(2,1)} async-done(((bf16[256,17920]{1,0:T(8,128)(2,1)}), bf16[32,17920]{1,0:T(8,128)(2,1)}) %reduce-scatter.3.cloned.1.call-update) | async-done | bytes 1146896 | tf_op jit(solution)/shard_map/reduce_scatter | solution.py:101
  229.9 1.6 slice_dynamic-update-slice_fusion.9
  231.5 1.6 slice_dynamic-update-slice_fusion.8
  233.1 3.6 %copy-done.13 = bf16[1280,3584]{1,0:T(8,128)(2,1)} copy-done((bf16[1280,3584]{1,0:T(8,128)(2,1)}, bf16[1280,3584]{1,0:T(8,128)(2,1)S(1)}, u32[]{:S(2)}) %copy-start.13) | copy-done | bytes 9175064
  236.7 2.8 reduce.2
  239.5 1.2 reshape.126
  240.6 10.2 %all-to-all-start.2 = ((bf16[32,2,8960]{2,1,0:T(2,128)(2,1)}), bf16[32,2,8960]{2,1,0:T(2,128)(2,1)S(1)}, u32[]{:S(2)}, u32[]{:S(2)}) async-start(bf16[32,2,8960]{2,1,0:T(2,128)(2,1)} %reshape.126), calls=%async_computation.3 | async-start | bytes 2293760 | tf_op jit(solution)/shard_map/all_to_all | solution.py:104
  250.9 2.9 slice_dynamic-update-slice_fusion.7
  253.8 3.0 slice_dynamic-update-slice_fusion.6
  256.7 2.9 slice_dynamic-update-slice_fusion.5
  259.6 18.9 %all-to-all-done.2 = bf16[32,2,8960]{2,1,0:T(2,128)(2,1)S(1)} async-done(((bf16[32,2,8960]{2,1,0:T(2,128)(2,1)}), bf16[32,2,8960]{2,1,0:T(2,128)(2,1)S(1)}, u32[]{:S(2)}, u32[]{:S(2)}) %all-to-all-start.2) | async-done | bytes 1146912 | tf_op jit(solution)/shard_map/all_to_all | solution.py:104
  278.6 3.4 reshape.127
  281.9 1.8 copy.46
  283.7 3.7 %all-gather.2.cloned.1.call-done = bf16[256,17920]{1,0:T(8,128)(2,1)} async-done(((bf16[32,17920]{1,0:T(8,128)(2,1)}), bf16[256,17920]{1,0:T(8,128)(2,1)}) %all-gather.2.cloned.1.call-update) | async-done | bytes 9175056 | tf_op jit(solution)/shard_map/all_gather | solution.py:103
  287.4 1.6 slice_dynamic-update-slice_fusion.4
  289.0 1.6 slice_dynamic-update-slice_fusion.3
  290.7 1.6 slice_dynamic-update-slice_fusion.2
  292.3 1.6 slice_dynamic-update-slice_fusion.1
  293.9 1.6 slice_dynamic-update-slice_fusion
  295.5 4.0 %fusion.10 = f32[1280,224]{0,1:T(8,128)} fusion(bf16[1280,3584]{1,0:T(8,128)(2,1)S(1)} %slice_dynamic-update-slice_fusion, bf16[1,224,3584]{2,1,0:T(8,128)(2,1)S(1)} %copy-done), kind=kOutput, calls=%fused_computation.30 | convolution fusion | flops 2055208960 | bytes 11927552 | tf_op jit(solution)/shard_map/dot_general | solution.py:107
  299.7 1.9 convolution_convert_fusion.9
  302.1 1.0 pad_maximum_fusion
  303.2 7.2 %fusion.7 = bf16[1,224,3584]{2,1,0:T(8,128)(2,1)} fusion(bf16[1280,224]{0,1:T(8,128)(2,1)S(1)} %multiply_convert_fusion.3, bf16[1280,3584]{1,0:T(8,128)(2,1)} %copy-done.14), kind=kOutput, calls=%fused_computation.17 | convolution fusion | flops 2056011776 | bytes 11354112 | tf_op jit(solution)/shard_map/dot_general | solution.py:114
  310.4 3.5 %fusion.6 = bf16[1,224,3584]{2,1,0:T(8,128)(2,1)} fusion(bf16[1280,3584]{1,0:T(8,128)(2,1)S(1)} %bitcast.127, f32[1280,224]{0,1:T(8,128)S(1)} %copy-done.18, f32[1280,224]{0,1:T(8,128)S(1)} %copy-done.7), kind=kOutput, calls=%fused_computation.16 | convolution fusion | flops 2057732096 | bytes 13074432 | tf_op jit(solution)/shard_map/dot_general | solution.py:116
  313.9 3.7 %fusion.5 = bf16[1,224,3584]{2,1,0:T(8,128)(2,1)} fusion(bf16[1280,3584]{1,0:T(8,128)(2,1)S(1)} %bitcast.127, f32[1280,224]{0,1:T(8,128)S(1)} %copy-done.7, f32[1280,224]{0,1:T(8,128)S(1)} %copy-done.18, f32[1280,224]{0,1:T(8,128)S(1)} %copy-done.5), kind=kOutput, calls=%fused_computation.15 | convolution fusion | flops 2058878976 | bytes 14221312 | tf_op jit(solution)/shard_map/dot_general | solution.py:115
  317.6 20.5 %reduce-scatter.5.cloned.1.call-done = bf16[16,3592]{1,0:T(8,128)(2,1)} async-done(((bf16[128,3592]{1,0:T(8,128)(2,1)}), bf16[16,3592]{1,0:T(8,128)(2,1)}) %reduce-scatter.5.cloned.1.call-update) | async-done | bytes 114960 | tf_op jit(solution)/shard_map/reduce_scatter | solution.py:126
  339.5 1.6 slice.155
  (100 shorter events, 15.9 us)
Async XLA Ops:
  7.2 157.7 %copy-start = (bf16[1,224,3584]{2,1,0:T(8,128)(2,1)S(1)}, bf16[1,224,3584]{2,1,0:T(8,128)(2,1)}, u32[]{:S(2)}) copy-start(bf16[1,224,3584]{2,1,0:T(8,128)(2,1)} %param.13) | copy-start | bytes 4816900
  7.2 2.0 copy-start.12
  9.7 1.0 copy-start.3
  15.2 11.9 %copy-start.15 = (f32[128,8]{0,1:T(8,128)S(1)}, f32[128,8]{0,1:T(8,128)}, u32[]{:S(2)}) copy-start(f32[128,8]{0,1:T(8,128)} %param.10) | copy-start | bytes 12292
  15.2 40.0 %all-to-all-start = ((bf16[32,2,8960]{2,1,0:T(2,128)(2,1)}), bf16[32,2,8960]{2,1,0:T(2,128)(2,1)S(1)}, u32[]{:S(2)}, u32[]{:S(2)}) async-start(bf16[32,2,8960]{2,1,0:T(2,128)(2,1)} %reshape.122), calls=%async_computation | async-start | bytes 2293760 | tf_op jit(solution)/shard_map/all_to_all | solution.py:50
  27.0 202.8 %reduce-scatter.3.cloned.1.call-start = ((), (), s32[]{:S(2)}) async-start(), calls=%async_computation.5 | async-start | bytes 10321920 | tf_op jit(solution)/shard_map/reduce_scatter | solution.py:101
  60.3 16.5 %collective-permute-start = (bf16[32,17920]{1,0:T(8,128)(2,1)S(1)}, bf16[32,17920]{1,0:T(8,128)(2,1)S(1)}, u32[]{:S(2)}, u32[]{:S(2)}) collective-permute-start(bf16[32,17920]{1,0:T(8,128)(2,1)S(1)} %bitcast.120), channel_id=1, source_target_pairs={{0,32},{32,64},{64,96},{96,128},{128,160},{160,192},{192,224},{224... | collective-permute-start | bytes 3440648 | tf_op jit(solution)/shard_map/ppermute | solution.py:59
  76.8 16.5 %copy-start.8 = (bf16[32,17920]{1,0:T(8,128)(2,1)}, bf16[32,17920]{1,0:T(8,128)(2,1)S(1)}, u32[]{:S(2)}) copy-start(bf16[32,17920]{1,0:T(8,128)(2,1)S(1)} %collective-permute-done) | copy-start | bytes 3440644
  76.8 16.5 %collective-permute-start.1 = (bf16[32,17920]{1,0:T(8,128)(2,1)S(1)}, bf16[32,17920]{1,0:T(8,128)(2,1)S(1)}, u32[]{:S(2)}, u32[]{:S(2)}) collective-permute-start(bf16[32,17920]{1,0:T(8,128)(2,1)S(1)} %collective-permute-done), channel_id=1, source_target_pairs={{0,32},{32,64},{64,96},{96,128},{128,160},{160,192},{192,224},{224... | collective-permute-start | bytes 3440648 | tf_op jit(solution)/shard_map/ppermute | solution.py:59
  76.8 16.5 %collective-permute-start.4 = (bf16[32,17920]{1,0:T(8,128)(2,1)S(1)}, bf16[32,17920]{1,0:T(8,128)(2,1)}, u32[]{:S(2)}, u32[]{:S(2)}) collective-permute-start(bf16[32,17920]{1,0:T(8,128)(2,1)S(1)} %bitcast.121), channel_id=1, source_target_pairs={{32,0},{64,32},{96,64},{128,96},{160,128},{192,160},{224,192},{0,2... | collective-permute-start | bytes 3440648 | tf_op jit(solution)/shard_map/ppermute | solution.py:61
  93.3 3.1 copy-start.10
  93.3 16.6 %collective-permute-start.2 = (bf16[32,17920]{1,0:T(8,128)(2,1)S(1)}, bf16[32,17920]{1,0:T(8,128)(2,1)}, u32[]{:S(2)}, u32[]{:S(2)}) collective-permute-start(bf16[32,17920]{1,0:T(8,128)(2,1)S(1)} %collective-permute-done.1), channel_id=1, source_target_pairs={{0,32},{32,64},{64,96},{96,128},{128,160},{160,192},{192,224},{224... | collective-permute-start | bytes 3440648 | tf_op jit(solution)/shard_map/ppermute | solution.py:59
  93.3 16.7 %collective-permute-start.5 = (bf16[32,17920]{1,0:T(8,128)(2,1)}, bf16[32,17920]{1,0:T(8,128)(2,1)}, u32[]{:S(2)}, u32[]{:S(2)}) collective-permute-start(bf16[32,17920]{1,0:T(8,128)(2,1)} %collective-permute-done.4), channel_id=1, source_target_pairs={{32,0},{64,32},{96,64},{128,96},{160,128},{192,160},{224,192},{0,2... | collective-permute-start | bytes 3440648 | tf_op jit(solution)/shard_map/ppermute | solution.py:61
  109.9 16.8 %collective-permute-start.3 = (bf16[32,17920]{1,0:T(8,128)(2,1)}, bf16[32,17920]{1,0:T(8,128)(2,1)}, u32[]{:S(2)}, u32[]{:S(2)}) collective-permute-start(bf16[32,17920]{1,0:T(8,128)(2,1)} %collective-permute-done.2), channel_id=1, source_target_pairs={{0,32},{32,64},{64,96},{96,128},{128,160},{160,192},{192,224},{224... | collective-permute-start | bytes 3440648 | tf_op jit(solution)/shard_map/ppermute | solution.py:59
  110.0 30.1 %collective-permute-start.6 = (bf16[32,17920]{1,0:T(8,128)(2,1)}, bf16[32,17920]{1,0:T(8,128)(2,1)S(1)}, u32[]{:S(2)}, u32[]{:S(2)}) collective-permute-start(bf16[32,17920]{1,0:T(8,128)(2,1)} %collective-permute-done.5), channel_id=1, source_target_pairs={{32,0},{64,32},{96,64},{128,96},{160,128},{192,160},{224,192},{0,2... | collective-permute-start | bytes 3440648 | tf_op jit(solution)/shard_map/ppermute | solution.py:61
  129.0 2.5 copy-start.11
  131.5 1.7 copy-start.9
  149.9 8.9 %copy-start.1 = (bf16[8,32,17920]{2,1,0:T(8,128)(2,1)S(1)}, bf16[8,32,17920]{2,1,0:T(8,128)(2,1)}, u32[]{:S(2)}) copy-start(bf16[8,32,17920]{2,1,0:T(8,128)(2,1)} %gather_fusion) | copy-start | bytes 27525124
  155.9 2.8 copy-start.16
  159.5 1.4 copy-start.17
  160.9 3.6 %copy-start.4 = (f32[1280,224]{0,1:T(8,128)}, f32[1280,224]{0,1:T(8,128)S(1)}, u32[]{:S(2)}) copy-start(f32[1280,224]{0,1:T(8,128)S(1)} %fusion.92) | copy-start | bytes 3440644
  164.5 2.3 copy-start.6
  174.5 112.9 %all-gather.2.cloned.1.call-start = ((), (), s32[]{:S(2)}) async-start(), calls=%async_computation.6 | async-start | bytes 10321920 | tf_op jit(solution)/shard_map/all_gather | solution.py:103
  233.1 3.6 %copy-start.13 = (bf16[1280,3584]{1,0:T(8,128)(2,1)}, bf16[1280,3584]{1,0:T(8,128)(2,1)S(1)}, u32[]{:S(2)}) copy-start(bf16[1280,3584]{1,0:T(8,128)(2,1)S(1)} %slice_dynamic-update-slice_fusion.8) | copy-start | bytes 27525124
  240.6 37.9 %all-to-all-start.2 = ((bf16[32,2,8960]{2,1,0:T(2,128)(2,1)}), bf16[32,2,8960]{2,1,0:T(2,128)(2,1)S(1)}, u32[]{:S(2)}, u32[]{:S(2)}) async-start(bf16[32,2,8960]{2,1,0:T(2,128)(2,1)} %reshape.126), calls=%async_computation.3 | async-start | bytes 2293760 | tf_op jit(solution)/shard_map/all_to_all | solution.py:104
  250.8 87.3 %reduce-scatter.5.cloned.1.call-start = ((), (), s32[]{:S(2)}) async-start(), calls=%async_computation.7 | async-start | bytes 1069056 | tf_op jit(solution)/shard_map/reduce_scatter | solution.py:126
  295.5 4.0 %copy-start.14 = (bf16[1280,3584]{1,0:T(8,128)(2,1)}, bf16[1280,3584]{1,0:T(8,128)(2,1)S(1)}, u32[]{:S(2)}) copy-start(bf16[1280,3584]{1,0:T(8,128)(2,1)S(1)} %slice_dynamic-update-slice_fusion) | copy-start | bytes 27525124
  299.6 1.9 copy-start.2
  303.1 7.2 %slice-start = ((s8[9175040]{0:T(1024)(128)(4,1)}), s8[786432]{0:T(1024)(128)(4,1)S(1)}, s32[]{:S(2)}) async-start(s8[9175040]{0:T(1024)(128)(4,1)} %bitcast.126), calls=%async_computation.8 | async-start | bytes 1572864
  303.2 7.2 %copy-start.7 = (f32[1280,224]{0,1:T(8,128)S(1)}, f32[1280,224]{0,1:T(8,128)}, u32[]{:S(2)}) copy-start(f32[1280,224]{0,1:T(8,128)} %copy-done.6) | copy-start | bytes 3440644
  303.2 7.2 %slice-start.1 = ((s8[9175040]{0:T(1024)(128)(4,1)}), s8[4194304]{0:T(1024)(128)(4,1)S(1)}, s32[]{:S(2)}) async-start(s8[9175040]{0:T(1024)(128)(4,1)} %bitcast.126), calls=%async_computation.9 | async-start | bytes 8388608
  303.2 7.2 %slice-start.2 = ((s8[9175040]{0:T(1024)(128)(4,1)}), s8[4194304]{0:T(1024)(128)(4,1)S(1)}, s32[]{:S(2)}) async-start(s8[9175040]{0:T(1024)(128)(4,1)} %bitcast.126), calls=%async_computation.10 | async-start | bytes 8388608
  303.2 7.2 %copy-start.18 = (f32[1280,224]{0,1:T(8,128)S(1)}, f32[1280,224]{0,1:T(8,128)}, u32[]{:S(2)}) copy-start(f32[1280,224]{0,1:T(8,128)} %fusion.10) | copy-start | bytes 3440644
  310.4 3.5 %copy-start.5 = (f32[1280,224]{0,1:T(8,128)S(1)}, f32[1280,224]{0,1:T(8,128)}, u32[]{:S(2)}) copy-start(f32[1280,224]{0,1:T(8,128)} %copy-done.4) | copy-start | bytes 3440644
Sparse Core Ops, SparseCore 0:
  174.6 55.1 reduce-scatter.2
  232.2 55.1 all-gather.1
  303.3 34.7 reduce-scatter.4
